TPU v7x, 128 devices: a whole 4x4x4 slice. The times are simulated.
128 devices in a mesh: px: 8 (over y, core), py: 16 (over z, x).
Axes of the slice: x: 4, y: 4, z: 4, core: 2. Of those that a mesh axis runs over, the one named last changes fastest.
Arguments:
- kappa: bfloat16 [301056, 128], P(('px', 'py')), may hold values from -6 to 6
- send_list: int32 [128, 128, 192], P(('px', 'py')), may hold values from 0 to 2351, as said below
- dest_slot: int32 [128, 128, 192], P(('px', 'py')), may hold values from 0 to 2047, as said below
- send_count: int32 [128, 128], P(('px', 'py')), may hold values from 0 to 192, as said below
Outputs:
- flexion: float32 [4, 4096, 8192], P(None, 'px', 'py')
Inputs may be any that keep to these rules, and one draw needn't show every extreme that they name: For k < send_count[a, d], send_list[a, d, k] is a row of source a's own 2352 tiles; later entries are 0. Over all sources a and k < send_count[a, d], dest_slot[a, d, k] names every slot of patch d exactly once; later entries are 0. send_count[a, d] is nonzero only where d's patch row equals a's px index or is one less; it is a multiple of 4, and reaches 192 in every draw. Summed over the sources a whose px index is one more than d's patch row, it is exactly 512.
All inputs are finite; a program needn't handle non-finite values.
Results may differ from a plain program's by a relative error of at most 0.0065.
Values may be sent and summed in bfloat16 or wider, within the bound.
No kernel may reach another device: no remote copies, remote signals or barrier semaphores. Data moves between devices by JAX's collectives and lax.ppermute only.
A program may use at most 64 MiB of HBM per device.

v0:
```python
import math
import jax
import jax.numpy as jnp
from jax import lax
from jax.sharding import PartitionSpec as P

PATCH_ROWS = 512
PATCH_COLS = 512


def shifted(shard, axis, by):
    size = lax.axis_size(axis)
    pairs = [(i, i + by) for i in range(size) if 0 <= i + by < size]
    return lax.ppermute(shard, axis, pairs)


def padded(block, sides, width):
    for axis, dim in sides:
        count = lax.axis_size(axis)
        forward = [(i, i + 1) for i in range(count - 1)]
        backward = [(target, source) for source, target in forward]
        low = lax.ppermute(
            lax.slice_in_dim(block, block.shape[dim] - width, None, axis=dim), axis, forward
        )
        high = lax.ppermute(lax.slice_in_dim(block, 0, width, axis=dim), axis, backward)
        block = jnp.concatenate([low, block, high], axis=dim)
    return block


def dft_tables(length):
    positions = jnp.arange(length, dtype=jnp.int32)
    phases = positions[:, None] * positions[None, :] % length
    angles = phases.astype(jnp.float32) * (2.0 * math.pi / length)
    return (jnp.cos(angles), jnp.sin(angles))


def wavenumbers(length):
    positions = jnp.arange(length, dtype=jnp.int32)
    signed = positions - length * (positions >= (length + 1) // 2).astype(jnp.int32)
    return signed.astype(jnp.float32) * (2.0 / length)


def flexion_fields(pixels):
    row_count = pixels.shape[0]
    col_count = pixels.shape[1]
    cos_cols, sin_cols = dft_tables(col_count)
    cos_rows, sin_rows = dft_tables(row_count)
    forward_cols = jnp.concatenate([cos_cols, sin_cols], axis=1).astype(jnp.bfloat16)
    halves = jnp.dot(pixels, forward_cols, preferred_element_type=jnp.float32)
    stacked = jnp.concatenate([halves[:, :col_count], halves[:, col_count:]], axis=0).astype(
        jnp.bfloat16
    )
    forward_rows = jnp.concatenate(
        [
            jnp.concatenate([cos_rows, -sin_rows], axis=1),
            jnp.concatenate([-sin_rows, -cos_rows], axis=1),
        ],
        axis=0,
    ).astype(jnp.bfloat16)
    spectrum = jnp.dot(forward_rows, stacked, preferred_element_type=jnp.float32)
    real_part = spectrum[:row_count]
    imag_part = spectrum[row_count:]
    across = wavenumbers(col_count)[None, :]
    down = wavenumbers(row_count)[:, None]
    scale = 1.0 / (row_count * col_count)
    power = across * across + down * down
    safe_power = jnp.where(power > 0, power, 1.0)
    cube_real = across * across * across - 3.0 * across * down * down
    cube_imag = 3.0 * across * across * down - down * down * down
    one_real = (-down * real_part - across * imag_part) * scale
    one_imag = (across * real_part - down * imag_part) * scale
    kernel_real = -cube_imag / safe_power
    kernel_imag = cube_real / safe_power
    three_real = (kernel_real * real_part - kernel_imag * imag_part) * scale
    three_imag = (kernel_real * imag_part + kernel_imag * real_part) * scale
    spectra = jnp.concatenate(
        [
            jnp.concatenate([one_real, three_real], axis=1),
            jnp.concatenate([one_imag, three_imag], axis=1),
        ],
        axis=0,
    ).astype(jnp.bfloat16)
    inverse_rows = jnp.concatenate(
        [
            jnp.concatenate([cos_rows, -sin_rows], axis=1),
            jnp.concatenate([sin_rows, cos_rows], axis=1),
        ],
        axis=0,
    ).astype(jnp.bfloat16)
    columns_done = jnp.dot(inverse_rows, spectra, preferred_element_type=jnp.float32).astype(
        jnp.bfloat16
    )
    arranged = jnp.concatenate(
        [
            jnp.concatenate(
                [columns_done[:row_count, :col_count], columns_done[row_count:, :col_count]], axis=1
            ),
            jnp.concatenate(
                [columns_done[:row_count, col_count:], columns_done[row_count:, col_count:]], axis=1
            ),
        ],
        axis=0,
    )
    inverse_cols = jnp.concatenate(
        [
            jnp.concatenate([cos_cols, sin_cols], axis=1),
            jnp.concatenate([-sin_cols, cos_cols], axis=1),
        ],
        axis=0,
    ).astype(jnp.bfloat16)
    result = jnp.dot(arranged, inverse_cols, preferred_element_type=jnp.float32)
    return jnp.stack(
        [
            result[:row_count, :col_count],
            result[:row_count, col_count:],
            result[row_count:, :col_count],
            result[row_count:, col_count:],
        ]
    ).astype(jnp.bfloat16)


def blend_edges(extended, has_top, has_bottom, has_left, has_right, width):
    values = extended.astype(jnp.float32)
    row_count = values.shape[1] - 2 * width
    col_count = values.shape[2] - 2 * width
    ramp = (jnp.arange(width, dtype=jnp.float32) + 0.5) / width
    top_weight = jnp.where(has_top, ramp, 1.0)[None, :, None]
    bottom_weight = jnp.where(has_bottom, ramp[::-1], 1.0)[None, :, None]
    middle = values[:, width : width + row_count, :]
    top_band = top_weight * middle[:, :width] + (1.0 - top_weight) * values[:, :width]
    bottom_band = (
        bottom_weight * middle[:, row_count - width :]
        + (1.0 - bottom_weight) * values[:, row_count + width :]
    )
    middle = jnp.concatenate([top_band, middle[:, width : row_count - width], bottom_band], axis=1)
    left_weight = jnp.where(has_left, ramp, 1.0)[None, None, :]
    right_weight = jnp.where(has_right, ramp[::-1], 1.0)[None, None, :]
    inner = middle[:, :, width : width + col_count]
    left_band = left_weight * inner[:, :, :width] + (1.0 - left_weight) * middle[:, :, :width]
    right_band = (
        right_weight * inner[:, :, col_count - width :]
        + (1.0 - right_weight) * middle[:, :, col_count + width :]
    )
    return jnp.concatenate([left_band, inner[:, :, width : col_count - width], right_band], axis=2)


def on_device(kappa, send_list, dest_slot, send_count):
    tile_width = kappa.shape[1]
    rows_axis = lax.axis_size("px")
    cols_axis = lax.axis_size("py")
    band_index = lax.axis_index("px")
    column_index = lax.axis_index("py")
    tile_lists = send_list[0].reshape(rows_axis, cols_axis, -1)
    slot_lists = dest_slot[0].reshape(rows_axis, cols_axis, -1)
    pair_counts = send_count[0].reshape(rows_axis, cols_axis)
    slot_depth = tile_lists.shape[2]
    upper_band = jnp.maximum(band_index - 1, 0)
    picked_lists = jnp.stack([tile_lists[band_index], tile_lists[upper_band]], axis=1)
    picked_slots = jnp.stack([slot_lists[band_index], slot_lists[upper_band]], axis=1)
    upper_counts = jnp.where(band_index > 0, pair_counts[upper_band], 0)
    picked_counts = jnp.stack([pair_counts[band_index], upper_counts], axis=1)
    live_mask = jnp.arange(slot_depth, dtype=jnp.int32)[None, None, :] < picked_counts[:, :, None]
    slot_codes = jnp.where(live_mask, picked_slots + 1, 0)
    whole_band, band_lists, band_codes = (
        lax.all_gather(kappa, "py", axis=0, tiled=True),
        lax.all_gather(picked_lists, "py", axis=0, tiled=True),
        lax.all_gather(slot_codes, "py", axis=0, tiled=True),
    )
    own_lists = band_lists.reshape(cols_axis, cols_axis, 2, slot_depth)[:, column_index]
    arrived_codes = band_codes.reshape(cols_axis, cols_axis, 2, slot_depth)[:, column_index]
    offsets = (jnp.arange(cols_axis, dtype=jnp.int32) * kappa.shape[0])[:, None, None]
    tile_values = whole_band[own_lists + offsets]
    raised_values, raised_codes = shifted((tile_values[:, 1], arrived_codes[:, 1]), "px", -1)
    all_values = jnp.concatenate(
        [tile_values[:, 0].reshape(-1, tile_width), raised_values.reshape(-1, tile_width)], axis=0
    )
    all_codes = jnp.concatenate([arrived_codes[:, 0].reshape(-1), raised_codes.reshape(-1)], axis=0)
    slot_total = PATCH_ROWS * PATCH_COLS // tile_width
    target = jnp.where(all_codes > 0, all_codes - 1, slot_total)
    patch_tiles = (
        jnp.zeros((slot_total, tile_width), kappa.dtype).at[target].set(all_values, mode="drop")
    )
    fields = flexion_fields(patch_tiles.reshape(PATCH_ROWS, PATCH_COLS))
    extended = padded(fields, (("px", 1), ("py", 2)), tile_width)
    return blend_edges(
        extended,
        band_index > 0,
        band_index < rows_axis - 1,
        column_index > 0,
        column_index < cols_axis - 1,
        tile_width,
    )


def solution(mesh):
    placed = (
        P(("px", "py"), None),
        P(("px", "py"), None, None),
        P(("px", "py"), None, None),
        P(("px", "py"), None),
    )
    return jax.shard_map(
        on_device, mesh=mesh, in_specs=placed, out_specs=P(None, "px", "py"), check_vma=False
    )
```

profile of v0, /device:TPU:15, one launch (start us, length us, event | category | flops | bytes accessed | tf_op | source)
XLA Modules:
  0.0 213.1 jit_solution(5844957314642020017)
XLA Ops:
  6.5 0.7 all-gather.2.cloned.1.call-update
  7.3 0.5 broadcast.420
  7.8 1.3 reduce.3
  9.2 1.0 copy.5
  10.2 1.0 copy.6
  11.3 21.8 %all_gather.9 = s32[256,2,192]{2,0,1:T(8,128)S(1)} all-gather(s32[16,2,192]{2,0,1:T(8,128)S(1)} %fusion.57), channel_id=1, replica_groups=mesh['px'=8,'py'=16] {'py'}, dimensions={0}, use_global_device_ids=true | all-gather | bytes 417792 | tf_op jit(solution)/shard_map/all_gather | solution.py:167
  33.1 6.5 %collective-permute-start = (s32[16,192]{1,0:T(8,128)S(1)}, s32[16,192]{1,0:T(8,128)S(1)}, u32[]{:S(2)}, u32[]{:S(2)}) collective-permute-start(s32[16,192]{1,0:T(8,128)S(1)} %get-tuple-element.41), channel_id=1, source_target_pairs={{16,0},{32,16},{48,32},{64,48},{80,64},{96,80},{112,96},{17,1},{33... | collective-permute-start | bytes 36872 | tf_op jit(solution)/shard_map/ppermute | solution.py:14
  39.8 18.9 %all_gather.11 = s32[256,2,192]{2,0,1:T(8,128)S(1)} all-gather(s32[16,2,192]{2,0,1:T(8,128)S(1)} %pad_add_fusion), channel_id=1, replica_groups=mesh['px'=8,'py'=16] {'py'}, dimensions={0}, use_global_device_ids=true | all-gather | bytes 417792 | tf_op jit(solution)/shard_map/all_gather | solution.py:166
  58.8 0.1 reshape.198
  58.9 4.0 %fusion.54 = bf16[512,512]{1,0:T(8,128)(2,1)S(1)} fusion(), kind=kLoop, calls=%fused_computation.93 | loop fusion | flops 4194304 | bytes 524288 | tf_op jit(solution)/shard_map/neg | solution.py:85
  62.9 4.3 %fusion.50 = (bf16[512,512]{1,0:T(8,128)(2,1)S(1)}, bf16[512,512]{1,0:T(8,128)(2,1)S(1)}) fusion(), kind=kLoop, calls=%fused_computation.89 | loop fusion | flops 4194304 | bytes 1048576 | tf_op jit(solution)/shard_map/sin | solution.py:34
  67.3 5.0 %negate_convert_fusion = (bf16[512,512]{1,0:T(8,128)(2,1)}, bf16[512,512]{1,0:T(8,128)(2,1)}) fusion(), kind=kLoop, calls=%fused_computation.70 | loop fusion | flops 4718592 | bytes 1048576 | tf_op jit(solution)/shard_map/convert.29
  72.3 5.0 %fusion.52 = (bf16[512,512]{1,0:T(8,128)(2,1)}, bf16[512,512]{1,0:T(8,128)(2,1)}) fusion(), kind=kLoop, calls=%fused_computation.91 | loop fusion | flops 4194304 | bytes 1048576 | tf_op jit(solution)/shard_map/convert.33
  77.2 1.2 fusion.2
  78.6 12.6 %all-gather.2.cloned.1.call-done = bf16[37632,128]{1,0:T(8,128)(2,1)} async-done(((bf16[2352,128]{1,0:T(8,128)(2,1)}), bf16[37632,128]{1,0:T(8,128)(2,1)}) %all-gather.2.cloned.1.call-update) | async-done | bytes 9633808 | tf_op jit(solution)/shard_map/all_gather | solution.py:165
  91.2 21.4 %gather_fusion = bf16[6144,128]{1,0:T(8,128)(2,1)S(1)} fusion(bf16[37632,128]{1,0:T(8,128)(2,1)} %all-gather.2.cloned.1.call-done, s32[6144]{0:T(1024)S(1)} %broadcast_clamp_fusion), kind=kCustom, calls=%fused_computation | custom fusion | bytes 3170304 | tf_op jit(solution)/shard_map/gather | solution.py:172
  112.7 0.1 fusion.71
  112.8 2.6 %collective-permute-start.1 = (bf16[16,192,128]{2,1,0:T(8,128)(2,1)S(1)}, bf16[16,192,128]{2,1,0:T(8,128)(2,1)S(1)}, u32[]{:S(2)}, u32[]{:S(2)}) collective-permute-start(bf16[16,192,128]{2,1,0:T(8,128)(2,1)S(1)} %get-tuple-element.32), channel_id=1, source_target_pairs={{16,0},{32,16},{48,32},{64,48},{80,64},{96,80},{112,96},{17,1},{33... | collective-permute-start | bytes 2359304 | tf_op jit(solution)/shard_map/ppermute | solution.py:14
  115.5 10.7 %collective-permute-done.1 = bf16[16,192,128]{2,1,0:T(8,128)(2,1)S(1)} collective-permute-done((bf16[16,192,128]{2,1,0:T(8,128)(2,1)S(1)}, bf16[16,192,128]{2,1,0:T(8,128)(2,1)S(1)}, u32[]{:S(2)}, u32[]{:S(2)}) %collective-permute-start.1) | collective-permute-done | bytes 786464 | tf_op jit(solution)/shard_map/ppermute | solution.py:14
  126.2 21.4 %scatter_custom_fusion = bf16[2048,128]{1,0:T(8,128)(2,1)S(1)} fusion(s32[6144]{0:T(1024)S(1)} %bitcast.53, bf16[3072,128]{1,0:T(8,128)(2,1)S(1)} %bitcast.47, bf16[]{:T(256)} %constant.88, bf16[3072,128]{1,0:T(8,128)(2,1)S(1)} %bitcast.46, bf16[]{:T(256)} %constant.24.clone.1), kind=kCustom, calls=%fused_computation.44 | custom fusion | flops 3145728 | bytes 2097156 | tf_op jit(solution)/shard_map/scatter | solution.py:181
  147.5 0.3 reshape.195
  147.9 0.7 convolution_convert_fusion
  148.7 0.4 copy-done
  149.1 0.1 copy-done.1
  149.2 0.2 copy-done.4
  149.4 1.3 fusion.1
  150.7 1.4 multiply_convert_fusion.3
  152.1 2.4 %fusion.29 = bf16[1024,1024]{0,1:T(8,128)(2,1)S(1)} fusion(bf16[512,512]{0,1:T(8,128)(2,1)S(1)} %get-tuple-element.19, bf16[512,512]{0,1:T(8,128)(2,1)S(1)} %get-tuple-element.18, bf16[512,512]{0,1:T(8,128)(2,1)S(1)} %get-tuple-element.20, bf16[512,512]{0,1:T(8,128)(2,1)S(1)} %get-tuple-element.17, bf16[512,1024]{1,0:T(8,128)(2,1)S(1)} %copy-done, ...), kind=kOutput, calls=%fused_computation.37 | convolution fusion | flops 2163212288 | bytes 6291456 | tf_op jit(solution)/shard_map/dot_general | solution.py:90
  154.5 0.2 fusion.70
  154.7 2.4 %fusion.24 = bf16[1024,1024]{1,0:T(8,128)(2,1)S(1)} fusion(bf16[512,512]{1,0:T(8,128)(2,1)S(1)} %copy-done.2, bf16[512,512]{1,0:T(8,128)(2,1)S(1)} %copy-done.1, bf16[512,1024]{1,0:T(8,128)(2,1)S(1)} %get-tuple-element.36, bf16[512,512]{0,1:T(8,128)(2,1)S(1)} %get-tuple-element.28, bf16[512,512]{0,1:T(8,128)(2,1)S(1)} %get-tuple-element.29, ...), kind=kOutput, calls=%fused_computation.36 | convolution fusion | flops 2163212288 | bytes 6291456 | tf_op jit(solution)/shard_map/dot_general | solution.py:111
  157.1 0.2 slice_bitcast_fusion.4
  157.4 1.9 collective-permute-start.2
  159.3 2.4 %collective-permute-start.3 = (bf16[4,128,512]{2,1,0:T(8,128)(2,1)S(1)}, bf16[4,128,512]{2,1,0:T(8,128)(2,1)S(1)}, u32[]{:S(2)}, u32[]{:S(2)}) collective-permute-start(bf16[4,128,512]{2,1,0:T(8,128)(2,1)S(1)} %get-tuple-element.22), channel_id=1, source_target_pairs={{16,0},{32,16},{48,32},{64,48},{80,64},{96,80},{112,96},{17,1},{33... | collective-permute-start | bytes 1572872 | tf_op jit(solution)/shard_map/ppermute | solution.py:25
  161.7 3.7 %collective-permute-done.2 = bf16[4,128,512]{2,1,0:T(8,128)(2,1)S(1)} collective-permute-done((bf16[4,128,512]{2,1,0:T(8,128)(2,1)S(1)}, bf16[4,128,512]{2,1,0:T(8,128)(2,1)S(1)}, u32[]{:S(2)}, u32[]{:S(2)}) %collective-permute-start.2) | collective-permute-done | bytes 524320 | tf_op jit(solution)/shard_map/ppermute | solution.py:22
  165.4 4.4 %collective-permute-done.3 = bf16[4,128,512]{2,1,0:T(8,128)(2,1)S(1)} collective-permute-done((bf16[4,128,512]{2,1,0:T(8,128)(2,1)S(1)}, bf16[4,128,512]{2,1,0:T(8,128)(2,1)S(1)}, u32[]{:S(2)}, u32[]{:S(2)}) %collective-permute-start.3) | collective-permute-done | bytes 524320 | tf_op jit(solution)/shard_map/ppermute | solution.py:25
  169.8 1.5 pad_maximum_fusion.20
  171.3 3.0 %collective-permute-start.4 = (bf16[4,768,128]{2,1,0:T(8,128)(2,1)}, bf16[4,768,128]{2,1,0:T(8,128)(2,1)}, u32[]{:S(2)}, u32[]{:S(2)}) collective-permute-start(bf16[4,768,128]{2,1,0:T(8,128)(2,1)} %get-tuple-element.13), channel_id=1, source_target_pairs={{0,1},{1,2},{2,3},{3,4},{4,5},{5,6},{6,7},{7,8},{8,9},{9,10},{10,1... | collective-permute-start | bytes 2359304 | tf_op jit(solution)/shard_map/ppermute | solution.py:22
  174.3 2.3 %collective-permute-start.5 = (bf16[4,768,128]{2,1,0:T(8,128)(2,1)}, bf16[4,768,128]{2,1,0:T(8,128)(2,1)}, u32[]{:S(2)}, u32[]{:S(2)}) collective-permute-start(bf16[4,768,128]{2,1,0:T(8,128)(2,1)} %get-tuple-element.14), channel_id=1, source_target_pairs={{1,0},{2,1},{3,2},{4,3},{5,4},{6,5},{7,6},{8,7},{9,8},{10,9},{11,1... | collective-permute-start | bytes 2359304 | tf_op jit(solution)/shard_map/ppermute | solution.py:25
  176.6 0.1 reverse.4
  176.7 15.5 %collective-permute-done.4 = bf16[4,768,128]{2,1,0:T(8,128)(2,1)} collective-permute-done((bf16[4,768,128]{2,1,0:T(8,128)(2,1)}, bf16[4,768,128]{2,1,0:T(8,128)(2,1)}, u32[]{:S(2)}, u32[]{:S(2)}) %collective-permute-start.4) | collective-permute-done | bytes 786464 | tf_op jit(solution)/shard_map/ppermute | solution.py:22
  192.2 5.2 %collective-permute-done.5 = bf16[4,768,128]{2,1,0:T(8,128)(2,1)} collective-permute-done((bf16[4,768,128]{2,1,0:T(8,128)(2,1)}, bf16[4,768,128]{2,1,0:T(8,128)(2,1)}, u32[]{:S(2)}, u32[]{:S(2)}) %collective-permute-start.5) | collective-permute-done | bytes 786464 | tf_op jit(solution)/shard_map/ppermute | solution.py:25
  197.4 4.6 %maximum_convert_fusion = f32[4,768,768]{2,1,0:T(8,128)S(1)} fusion(bf16[4,768,128]{2,1,0:T(8,128)(2,1)} %collective-permute-done.5, bf16[4,128,512]{2,1,0:T(8,128)(2,1)S(1)} %collective-permute-done.3, bf16[1,512,512]{2,1,0:T(8,128)(2,1)S(1)} %get-tuple-element.24, bf16[1,512,512]{2,1,0:T(8,128)(2,1)S(1)} %get-tuple-element.25, ...), kind=kLoop, calls=%fused_computation.3 | loop fusion | flops 37748736 | bytes 14155776 | tf_op jit(solution)/shard_map/convert_element_type | solution.py:123
  202.0 0.2 slice.154
  202.2 0.5 fusion.33
  202.7 0.6 pad_maximum_fusion
  203.3 0.1 slice.157
  203.5 0.2 fusion.42
  203.7 2.5 %pad_maximum_fusion.1 = f32[4,512,512]{2,1,0:T(8,128)} fusion(f32[4,512,128]{2,1,0:T(8,128)S(1)} %get-tuple-element.12, f32[4,512,256]{2,1,0:T(8,128)S(1)} %slice.157, f32[4,512,128]{2,1,0:T(8,128)S(1)} %get-tuple-element.11), kind=kLoop, calls=%fused_computation.4 | loop fusion | flops 2097152 | bytes 8388608 | tf_op jit(solution)/shard_map/concatenate | solution.py:144
  (37 shorter events, 0.8 us)
Async XLA Ops:
  6.5 84.7 %all-gather.2.cloned.1.call-start = ((), (), s32[]{:S(2)}) async-start(), calls=%async_computation | async-start | bytes 10235904 | tf_op jit(solution)/shard_map/all_gather | solution.py:165
  33.1 45.4 %collective-permute-start = (s32[16,192]{1,0:T(8,128)S(1)}, s32[16,192]{1,0:T(8,128)S(1)}, u32[]{:S(2)}, u32[]{:S(2)}) collective-permute-start(s32[16,192]{1,0:T(8,128)S(1)} %get-tuple-element.41), channel_id=1, source_target_pairs={{16,0},{32,16},{48,32},{64,48},{80,64},{96,80},{112,96},{17,1},{33... | collective-permute-start | bytes 36872 | tf_op jit(solution)/shard_map/ppermute | solution.py:14
  112.8 13.4 %collective-permute-start.1 = (bf16[16,192,128]{2,1,0:T(8,128)(2,1)S(1)}, bf16[16,192,128]{2,1,0:T(8,128)(2,1)S(1)}, u32[]{:S(2)}, u32[]{:S(2)}) collective-permute-start(bf16[16,192,128]{2,1,0:T(8,128)(2,1)S(1)} %get-tuple-element.32), channel_id=1, source_target_pairs={{16,0},{32,16},{48,32},{64,48},{80,64},{96,80},{112,96},{17,1},{33... | collective-permute-start | bytes 2359304 | tf_op jit(solution)/shard_map/ppermute | solution.py:14
  147.9 1.2 copy-start
  147.9 1.3 copy-start.1
  147.9 1.5 copy-start.4
  150.7 1.4 copy-start.2
  150.7 1.4 copy-start.3
  157.4 8.0 %collective-permute-start.2 = (bf16[4,128,512]{2,1,0:T(8,128)(2,1)S(1)}, bf16[4,128,512]{2,1,0:T(8,128)(2,1)S(1)}, u32[]{:S(2)}, u32[]{:S(2)}) collective-permute-start(bf16[4,128,512]{2,1,0:T(8,128)(2,1)S(1)} %get-tuple-element.21), channel_id=1, source_target_pairs={{0,16},{16,32},{32,48},{48,64},{64,80},{80,96},{96,112},{1,17},{17... | collective-permute-start | bytes 1572872 | tf_op jit(solution)/shard_map/ppermute | solution.py:22
  159.3 10.5 %collective-permute-start.3 = (bf16[4,128,512]{2,1,0:T(8,128)(2,1)S(1)}, bf16[4,128,512]{2,1,0:T(8,128)(2,1)S(1)}, u32[]{:S(2)}, u32[]{:S(2)}) collective-permute-start(bf16[4,128,512]{2,1,0:T(8,128)(2,1)S(1)} %get-tuple-element.22), channel_id=1, source_target_pairs={{16,0},{32,16},{48,32},{64,48},{80,64},{96,80},{112,96},{17,1},{33... | collective-permute-start | bytes 1572872 | tf_op jit(solution)/shard_map/ppermute | solution.py:25
  171.3 21.0 %collective-permute-start.4 = (bf16[4,768,128]{2,1,0:T(8,128)(2,1)}, bf16[4,768,128]{2,1,0:T(8,128)(2,1)}, u32[]{:S(2)}, u32[]{:S(2)}) collective-permute-start(bf16[4,768,128]{2,1,0:T(8,128)(2,1)} %get-tuple-element.13), channel_id=1, source_target_pairs={{0,1},{1,2},{2,3},{3,4},{4,5},{5,6},{6,7},{7,8},{8,9},{9,10},{10,1... | collective-permute-start | bytes 2359304 | tf_op jit(solution)/shard_map/ppermute | solution.py:22
  174.3 23.1 %collective-permute-start.5 = (bf16[4,768,128]{2,1,0:T(8,128)(2,1)}, bf16[4,768,128]{2,1,0:T(8,128)(2,1)}, u32[]{:S(2)}, u32[]{:S(2)}) collective-permute-start(bf16[4,768,128]{2,1,0:T(8,128)(2,1)} %get-tuple-element.14), channel_id=1, source_target_pairs={{1,0},{2,1},{3,2},{4,3},{5,4},{6,5},{7,6},{8,7},{9,8},{10,9},{11,1... | collective-permute-start | bytes 2359304 | tf_op jit(solution)/shard_map/ppermute | solution.py:25
Sparse Core Ops, SparseCore 0:
  9.5 81.6 all-gather.1
where the time goes:
time: 214 us; the launch traced here: 213 us
  other arithmetic  53.8 us (25%)
  waiting for transfers between devices  52.8 us (25%)
  blocking collectives  40.7 us (19%)
  local copies, waits for them, and re-layouts  26.4 us (12%)
  starting transfers between devices  18.7 us (9%)
  between operations  13.8 us (6%)
  matrix products  6.84 us (3%)
    all_gather x1, blocking collectives, on_device(): lax.all_gather(slot_codes, 'py', axis=0, tiled=True)  21.8 us
    gather x1, local copies, waits for them, and re-layouts, on_device(): tile_values = whole_band[own_lists + offsets]  21.4 us
    scatter x1, other arithmetic, on_device(): jnp.zeros((slot_total, tile_width), kappa.dtype).at[target]  21.4 us
    ppermute x2, waiting for transfers between devices, padded(): lax.ppermute(lax.slice_in_dim(block, block.shape[dim] - width, None, axis...  19.2 us
    all_gather x1, blocking collectives, on_device(): lax.all_gather(picked_lists, 'py', axis=0, tiled=True)  18.9 us
    all_gather x1, waiting for transfers between devices, on_device(): lax.all_gather(kappa, 'py', axis=0, tiled=True)  12.6 us
    another operation x4, other arithmetic  12.6 us
    ppermute x2, waiting for transfers between devices, shifted(): return lax.ppermute(shard, axis, pairs)  10.7 us
  transfers between devices with their start and end apart: 7, of which 6 were waited for; matrix products, arithmetic and copies ran while one was open for 11% of the time, Pallas kernels for 0%

commit v1 on v0

--- a/solution.py
+++ b/solution.py
@@ -162,7 +162,9 @@
     live_mask = jnp.arange(slot_depth, dtype=jnp.int32)[None, None, :] < picked_counts[:, :, None]
     slot_codes = jnp.where(live_mask, picked_slots + 1, 0)
     whole_band, band_lists, band_codes = (
-        lax.all_gather(kappa, "py", axis=0, tiled=True),
+        jnp.concatenate(
+            lax.all_to_all(jnp.stack([kappa] * lax.axis_size("py")), "py", 0, 0), axis=0
+        ),
         lax.all_gather(picked_lists, "py", axis=0, tiled=True),
         lax.all_gather(slot_codes, "py", axis=0, tiled=True),
     )

time: 214 us -> 332 us (1.55)
  blocking collectives: 40.7 us -> 168 us
  between operations: 13.8 us -> 0.42 us
  starting transfers between devices: 18.7 us -> 31.9 us
  waiting for transfers between devices: 52.8 us -> 39.8 us
  local copies, waits for them, and re-layouts: 26.4 us -> 30.7 us
    all_gather x1, blocking collectives: 21.8 us -> 151 us  [on_device(): lax.all_gather(slot_codes, 'py', axis=0, tiled=True)]
    all_gather x1 -> x0, waiting for transfers between devices: 12.6 us -> none  [on_device(): lax.all_gather(kappa, 'py', axis=0, tiled=True)]
    all_to_all x0 -> x1, starting transfers between devices: none -> 7.84 us  [on_device(): lax.all_to_all(jnp.stack([kappa] * lax.axis_size('py')), 'py', 0, 0)]
    another operation x1 -> x2, local copies, waits for them, and re-layouts: 0.1 us -> 6.12 us  [the longest x1 6.02 us: on_device(): jnp.stack([kappa] * lax.axis_size('py'))]
    ppermute x2, starting transfers between devices: 9.14 us -> 14.2 us  [shifted(): return lax.ppermute(shard, axis, pairs)]
  transfers between devices with their start and end apart: 7 -> 7, of which waited for: 6 -> 5; matrix products, arithmetic and copies ran while one was open for 11% -> 7% of each run, Pallas kernels for 0% -> 0%
where the time goes in v1:
time: 332 us; the launch traced here: 331 us
  blocking collectives  168 us (51%)
  other arithmetic  53.1 us (16%)
  waiting for transfers between devices  39.8 us (12%)
  starting transfers between devices  31.9 us (10%)
  local copies, waits for them, and re-layouts  30.7 us (9%)
  matrix products  6.84 us (2%)
    all_gather x1, blocking collectives, on_device(): lax.all_gather(slot_codes, 'py', axis=0, tiled=True)  151 us
    gather x1, local copies, waits for them, and re-layouts, on_device(): tile_values = whole_band[own_lists + offsets]  21.4 us
    scatter x1, other arithmetic, on_device(): jnp.zeros((slot_total, tile_width), kappa.dtype).at[target]  21.4 us
    ppermute x2, waiting for transfers between devices, padded(): lax.ppermute(lax.slice_in_dim(block, block.shape[dim] - width, None, axis...  18.8 us
    all_gather x1, blocking collectives, on_device(): lax.all_gather(picked_lists, 'py', axis=0, tiled=True)  16.9 us
    ppermute x2, starting transfers between devices, shifted(): return lax.ppermute(shard, axis, pairs)  14.2 us
    another operation x4, other arithmetic  12.6 us
    ppermute x2, waiting for transfers between devices, shifted(): return lax.ppermute(shard, axis, pairs)  10.8 us
  transfers between devices with their start and end apart: 7, of which 5 were waited for; matrix products, arithmetic and copies ran while one was open for 7% of the time, Pallas kernels for 0%

profile of v1, /device:TPU:15, one launch (start us, length us, event | category | flops | bytes accessed | tf_op | source)
XLA Modules:
  0.0 331.0 jit_solution(5312031852067562438)
XLA Ops:
  0.0 6.0 %stack.25 = bf16[16,2352,128]{2,1,0:T(8,128)(2,1)} broadcast(bf16[2352,128]{1,0:T(8,128)(2,1)} %param.4), dimensions={1,2} | broadcast | bytes 10235904 | tf_op jit(solution)/shard_map/stack | solution.py:166
  6.0 7.8 %all-to-all-start = ((bf16[16,2352,128]{2,1,0:T(8,128)(2,1)}), bf16[16,2352,128]{2,1,0:T(8,128)(2,1)}, u32[]{:S(2)}, u32[]{:S(2)}) async-start(bf16[16,2352,128]{2,1,0:T(8,128)(2,1)} %stack.25), calls=%async_computation | async-start | bytes 19267584 | tf_op jit(solution)/shard_map/all_to_all | solution.py:166
  13.9 0.5 broadcast.422
  14.4 0.7 reduce.3
  15.1 0.1 copy.5
  15.2 0.1 copy.6
  15.5 151.3 %all_gather.6 = s32[256,2,192]{2,0,1:T(8,128)S(1)} all-gather(s32[16,2,192]{2,0,1:T(8,128)S(1)} %fusion.57), channel_id=1, replica_groups=mesh['px'=8,'py'=16] {'py'}, dimensions={0}, use_global_device_ids=true | all-gather | bytes 417792 | tf_op jit(solution)/shard_map/all_gather | solution.py:169
  166.8 7.1 %collective-permute-start = (s32[16,192]{1,0:T(8,128)S(1)}, s32[16,192]{1,0:T(8,128)S(1)}, u32[]{:S(2)}, u32[]{:S(2)}) collective-permute-start(s32[16,192]{1,0:T(8,128)S(1)} %get-tuple-element.41), channel_id=1, source_target_pairs={{16,0},{32,16},{48,32},{64,48},{80,64},{96,80},{112,96},{17,1},{33... | collective-permute-start | bytes 36872 | tf_op jit(solution)/shard_map/ppermute | solution.py:14
  174.0 16.9 %all_gather.7 = s32[256,2,192]{2,0,1:T(8,128)S(1)} all-gather(s32[16,2,192]{2,0,1:T(8,128)S(1)} %pad_add_fusion), channel_id=1, replica_groups=mesh['px'=8,'py'=16] {'py'}, dimensions={0}, use_global_device_ids=true | all-gather | bytes 417792 | tf_op jit(solution)/shard_map/all_gather | solution.py:168
  191.1 0.1 reshape.204
  191.2 4.0 %fusion.54 = bf16[512,512]{1,0:T(8,128)(2,1)S(1)} fusion(), kind=kLoop, calls=%fused_computation.93 | loop fusion | flops 4194304 | bytes 524288 | tf_op jit(solution)/shard_map/neg | solution.py:85
  195.2 4.3 %fusion.50 = (bf16[512,512]{1,0:T(8,128)(2,1)S(1)}, bf16[512,512]{1,0:T(8,128)(2,1)S(1)}) fusion(), kind=kLoop, calls=%fused_computation.89 | loop fusion | flops 4194304 | bytes 1048576 | tf_op jit(solution)/shard_map/sin | solution.py:34
  199.5 5.0 %negate_convert_fusion = (bf16[512,512]{1,0:T(8,128)(2,1)}, bf16[512,512]{1,0:T(8,128)(2,1)}) fusion(), kind=kLoop, calls=%fused_computation.70 | loop fusion | flops 4718592 | bytes 1048576 | tf_op jit(solution)/shard_map/convert.29
  204.6 5.0 %fusion.52 = (bf16[512,512]{1,0:T(8,128)(2,1)}, bf16[512,512]{1,0:T(8,128)(2,1)}) fusion(), kind=kLoop, calls=%fused_computation.91 | loop fusion | flops 4194304 | bytes 1048576 | tf_op jit(solution)/shard_map/convert.33
  209.5 1.2 fusion.2
  210.9 21.4 %gather_fusion = bf16[6144,128]{1,0:T(8,128)(2,1)S(1)} fusion(bf16[37632,128]{1,0:T(8,128)(2,1)} %bitcast.8, s32[6144]{0:T(1024)S(1)} %broadcast_clamp_fusion), kind=kCustom, calls=%fused_computation | custom fusion | bytes 3170304 | tf_op jit(solution)/shard_map/gather | solution.py:174
  232.3 0.1 fusion.71
  232.4 7.1 %collective-permute-start.1 = (bf16[16,192,128]{2,1,0:T(8,128)(2,1)S(1)}, bf16[16,192,128]{2,1,0:T(8,128)(2,1)S(1)}, u32[]{:S(2)}, u32[]{:S(2)}) collective-permute-start(bf16[16,192,128]{2,1,0:T(8,128)(2,1)S(1)} %get-tuple-element.32), channel_id=1, source_target_pairs={{16,0},{32,16},{48,32},{64,48},{80,64},{96,80},{112,96},{17,1},{33... | collective-permute-start | bytes 2359304 | tf_op jit(solution)/shard_map/ppermute | solution.py:14
  239.6 10.8 %collective-permute-done.1 = bf16[16,192,128]{2,1,0:T(8,128)(2,1)S(1)} collective-permute-done((bf16[16,192,128]{2,1,0:T(8,128)(2,1)S(1)}, bf16[16,192,128]{2,1,0:T(8,128)(2,1)S(1)}, u32[]{:S(2)}, u32[]{:S(2)}) %collective-permute-start.1) | collective-permute-done | bytes 786464 | tf_op jit(solution)/shard_map/ppermute | solution.py:14
  250.4 21.4 %scatter_custom_fusion = bf16[2048,128]{1,0:T(8,128)(2,1)S(1)} fusion(s32[6144]{0:T(1024)S(1)} %bitcast.54, bf16[3072,128]{1,0:T(8,128)(2,1)S(1)} %bitcast.48, bf16[]{:T(256)} %constant.88, bf16[3072,128]{1,0:T(8,128)(2,1)S(1)} %bitcast.47, bf16[]{:T(256)} %constant.24.clone.1), kind=kCustom, calls=%fused_computation.44 | custom fusion | flops 3145728 | bytes 2097156 | tf_op jit(solution)/shard_map/scatter | solution.py:183
  271.7 0.3 reshape.201
  272.1 0.7 convolution_convert_fusion
  272.9 0.4 copy-done
  273.3 0.1 copy-done.1
  273.4 0.2 copy-done.4
  273.6 1.3 fusion.1
  274.9 1.4 multiply_convert_fusion.3
  276.3 2.4 fusion.29
  278.7 0.2 fusion.70
  278.9 2.4 fusion.24
  281.3 0.2 slice_bitcast_fusion.4
  281.6 1.9 collective-permute-start.2
  283.5 2.4 collective-permute-start.3
  285.9 3.7 %collective-permute-done.2 = bf16[4,128,512]{2,1,0:T(8,128)(2,1)S(1)} collective-permute-done((bf16[4,128,512]{2,1,0:T(8,128)(2,1)S(1)}, bf16[4,128,512]{2,1,0:T(8,128)(2,1)S(1)}, u32[]{:S(2)}, u32[]{:S(2)}) %collective-permute-start.2) | collective-permute-done | bytes 524320 | tf_op jit(solution)/shard_map/ppermute | solution.py:22
  289.6 4.4 %collective-permute-done.3 = bf16[4,128,512]{2,1,0:T(8,128)(2,1)S(1)} collective-permute-done((bf16[4,128,512]{2,1,0:T(8,128)(2,1)S(1)}, bf16[4,128,512]{2,1,0:T(8,128)(2,1)S(1)}, u32[]{:S(2)}, u32[]{:S(2)}) %collective-permute-start.3) | collective-permute-done | bytes 524320 | tf_op jit(solution)/shard_map/ppermute | solution.py:25
  294.0 1.5 pad_maximum_fusion.20
  295.5 3.7 %collective-permute-start.4 = (bf16[4,768,128]{2,1,0:T(8,128)(2,1)}, bf16[4,768,128]{2,1,0:T(8,128)(2,1)}, u32[]{:S(2)}, u32[]{:S(2)}) collective-permute-start(bf16[4,768,128]{2,1,0:T(8,128)(2,1)} %get-tuple-element.13), channel_id=1, source_target_pairs={{0,1},{1,2},{2,3},{3,4},{4,5},{5,6},{6,7},{7,8},{8,9},{9,10},{10,1... | collective-permute-start | bytes 2359304 | tf_op jit(solution)/shard_map/ppermute | solution.py:22
  299.2 1.9 collective-permute-start.5
  301.1 0.1 reverse.4
  301.2 15.1 %collective-permute-done.4 = bf16[4,768,128]{2,1,0:T(8,128)(2,1)} collective-permute-done((bf16[4,768,128]{2,1,0:T(8,128)(2,1)}, bf16[4,768,128]{2,1,0:T(8,128)(2,1)}, u32[]{:S(2)}, u32[]{:S(2)}) %collective-permute-start.4) | collective-permute-done | bytes 786464 | tf_op jit(solution)/shard_map/ppermute | solution.py:22
  316.3 5.8 %collective-permute-done.5 = bf16[4,768,128]{2,1,0:T(8,128)(2,1)} collective-permute-done((bf16[4,768,128]{2,1,0:T(8,128)(2,1)}, bf16[4,768,128]{2,1,0:T(8,128)(2,1)}, u32[]{:S(2)}, u32[]{:S(2)}) %collective-permute-start.5) | collective-permute-done | bytes 786464 | tf_op jit(solution)/shard_map/ppermute | solution.py:25
  322.1 4.6 %maximum_convert_fusion = f32[4,768,768]{2,1,0:T(8,128)S(1)} fusion(bf16[4,768,128]{2,1,0:T(8,128)(2,1)} %collective-permute-done.5, bf16[4,128,512]{2,1,0:T(8,128)(2,1)S(1)} %collective-permute-done.3, bf16[1,512,512]{2,1,0:T(8,128)(2,1)S(1)} %get-tuple-element.24, bf16[1,512,512]{2,1,0:T(8,128)(2,1)S(1)} %get-tuple-element.25, ...), kind=kLoop, calls=%fused_computation.3 | loop fusion | flops 37748736 | bytes 14155776 | tf_op jit(solution)/shard_map/convert_element_type | solution.py:123
  326.7 0.2 slice.154
  327.0 0.5 fusion.33
  327.5 0.6 pad_maximum_fusion
  328.1 0.1 slice.157
  328.2 0.2 fusion.42
  328.5 2.5 pad_maximum_fusion.1
  (43 shorter events, 0.8 us)
Async XLA Ops:
  6.0 8.4 %copy-start.7 = (s32[1,128]{1,0:T(1,128)S(1)}, s32[1,128]{1,0:T(1,128)}, u32[]{:S(2)}) copy-start(s32[1,128]{1,0:T(1,128)} %param.7) | copy-start | bytes 1540
  6.0 9.1 %copy-start.5 = (s32[1,128,192]{1,2,0:T(8,128)S(1)}, s32[1,128,192]{1,2,0:T(8,128)}, u32[]{:S(2)}) copy-start(s32[1,128,192]{1,2,0:T(8,128)} %param.6) | copy-start | bytes 294916
  6.0 9.2 %copy-start.6 = (s32[1,128,192]{1,2,0:T(8,128)S(1)}, s32[1,128,192]{1,2,0:T(8,128)}, u32[]{:S(2)}) copy-start(s32[1,128,192]{1,2,0:T(8,128)} %param.5) | copy-start | bytes 294916
  6.0 204.9 %all-to-all-start = ((bf16[16,2352,128]{2,1,0:T(8,128)(2,1)}), bf16[16,2352,128]{2,1,0:T(8,128)(2,1)}, u32[]{:S(2)}, u32[]{:S(2)}) async-start(bf16[16,2352,128]{2,1,0:T(8,128)(2,1)} %stack.25), calls=%async_computation | async-start | bytes 19267584 | tf_op jit(solution)/shard_map/all_to_all | solution.py:166
  166.8 43.9 %collective-permute-start = (s32[16,192]{1,0:T(8,128)S(1)}, s32[16,192]{1,0:T(8,128)S(1)}, u32[]{:S(2)}, u32[]{:S(2)}) collective-permute-start(s32[16,192]{1,0:T(8,128)S(1)} %get-tuple-element.41), channel_id=1, source_target_pairs={{16,0},{32,16},{48,32},{64,48},{80,64},{96,80},{112,96},{17,1},{33... | collective-permute-start | bytes 36872 | tf_op jit(solution)/shard_map/ppermute | solution.py:14
  232.4 17.9 %collective-permute-start.1 = (bf16[16,192,128]{2,1,0:T(8,128)(2,1)S(1)}, bf16[16,192,128]{2,1,0:T(8,128)(2,1)S(1)}, u32[]{:S(2)}, u32[]{:S(2)}) collective-permute-start(bf16[16,192,128]{2,1,0:T(8,128)(2,1)S(1)} %get-tuple-element.32), channel_id=1, source_target_pairs={{16,0},{32,16},{48,32},{64,48},{80,64},{96,80},{112,96},{17,1},{33... | collective-permute-start | bytes 2359304 | tf_op jit(solution)/shard_map/ppermute | solution.py:14
  272.1 1.2 copy-start
  272.1 1.3 copy-start.1
  272.1 1.5 copy-start.4
  274.9 1.4 copy-start.2
  274.9 1.4 copy-start.3
  281.6 8.0 %collective-permute-start.2 = (bf16[4,128,512]{2,1,0:T(8,128)(2,1)S(1)}, bf16[4,128,512]{2,1,0:T(8,128)(2,1)S(1)}, u32[]{:S(2)}, u32[]{:S(2)}) collective-permute-start(bf16[4,128,512]{2,1,0:T(8,128)(2,1)S(1)} %get-tuple-element.21), channel_id=1, source_target_pairs={{0,16},{16,32},{32,48},{48,64},{64,80},{80,96},{96,112},{1,17},{17... | collective-permute-start | bytes 1572872 | tf_op jit(solution)/shard_map/ppermute | solution.py:22
  283.5 10.5 %collective-permute-start.3 = (bf16[4,128,512]{2,1,0:T(8,128)(2,1)S(1)}, bf16[4,128,512]{2,1,0:T(8,128)(2,1)S(1)}, u32[]{:S(2)}, u32[]{:S(2)}) collective-permute-start(bf16[4,128,512]{2,1,0:T(8,128)(2,1)S(1)} %get-tuple-element.22), channel_id=1, source_target_pairs={{16,0},{32,16},{48,32},{64,48},{80,64},{96,80},{112,96},{17,1},{33... | collective-permute-start | bytes 1572872 | tf_op jit(solution)/shard_map/ppermute | solution.py:25
  295.5 20.9 %collective-permute-start.4 = (bf16[4,768,128]{2,1,0:T(8,128)(2,1)}, bf16[4,768,128]{2,1,0:T(8,128)(2,1)}, u32[]{:S(2)}, u32[]{:S(2)}) collective-permute-start(bf16[4,768,128]{2,1,0:T(8,128)(2,1)} %get-tuple-element.13), channel_id=1, source_target_pairs={{0,1},{1,2},{2,3},{3,4},{4,5},{5,6},{6,7},{7,8},{8,9},{9,10},{10,1... | collective-permute-start | bytes 2359304 | tf_op jit(solution)/shard_map/ppermute | solution.py:22
  299.2 23.0 %collective-permute-start.5 = (bf16[4,768,128]{2,1,0:T(8,128)(2,1)}, bf16[4,768,128]{2,1,0:T(8,128)(2,1)}, u32[]{:S(2)}, u32[]{:S(2)}) collective-permute-start(bf16[4,768,128]{2,1,0:T(8,128)(2,1)} %get-tuple-element.14), channel_id=1, source_target_pairs={{1,0},{2,1},{3,2},{4,3},{5,4},{6,5},{7,6},{8,7},{9,8},{10,9},{11,1... | collective-permute-start | bytes 2359304 | tf_op jit(solution)/shard_map/ppermute | solution.py:25
